TPU v7x, 128 devices: a whole 4x4x4 slice. The times are simulated.
128 devices in a mesh: expert: 32 (over y, z, core), dp: 4 (over x).
Axes of the slice: x: 4, y: 4, z: 4, core: 2. Of those that a mesh axis runs over, the one named last changes fastest.
Arguments:
- activations: bfloat16 [2048, 7168], P(('expert', 'dp')), may hold values from -6 to 6
- cotangent: bfloat16 [2048, 7168], P(('expert', 'dp')), may hold values from -6 to 6
- route_ids: int32 [2048, 8], P(('expert', 'dp')), may hold values from 0 to 31, all different within a row; in each aligned block of 16 rows (0 to 15, 16 to 31, ...) at most 5 rows name the same one
- route_weights: float32 [2048, 8], P(('expert', 'dp')), may hold values from 0.05 to 0.6
- gate_weights: bfloat16 [32, 7168, 1024], P('expert', 'dp'), may hold values from -0.0625 to 0.0625
- up_weights: bfloat16 [32, 7168, 1024], P('expert', 'dp'), may hold values from -0.0625 to 0.0625
- down_weights: bfloat16 [32, 1024, 7168], P('expert', None, 'dp'), may hold values from -0.1875 to 0.1875
Outputs:
- grad_input: bfloat16 [2048, 7168], P(('expert', 'dp'))
- grad_gate: bfloat16 [32, 7168, 1024], P('expert', 'dp')
- grad_up: bfloat16 [32, 7168, 1024], P('expert', 'dp')
- grad_down: bfloat16 [32, 1024, 7168], P('expert', None, 'dp')
Inputs may be any that keep to these rules, and one draw needn't show every extreme that they name: `route_ids`: each token names 8 different experts. Among the routes of one device's 16 tokens, no expert is named more than 5 times, a bound that some block reaches.
All inputs are finite; a program needn't handle non-finite values.
Results may differ from a plain program's by a relative error of at most 0.0064.
Values may be sent and summed in bfloat16 or wider, within the bound.
No kernel may reach another device: no remote copies, remote signals or barrier semaphores. Data moves between devices by JAX's collectives and lax.ppermute only.
A program may use at most 128 MiB of HBM per device.

v0:
```python
import jax
import jax.numpy as jnp
from jax import lax
from jax.sharding import PartitionSpec as P


def swiglu_back(gate, upper, upstream):
    sigma = jax.nn.sigmoid(gate)
    silu_gate = gate * sigma
    activated = (silu_gate * upper).astype(jnp.bfloat16)
    grad_pre = (upstream * upper * sigma * (1.0 + gate * (1.0 - sigma))).astype(jnp.bfloat16)
    grad_lin = (upstream * silu_gate).astype(jnp.bfloat16)
    return (grad_pre, grad_lin, activated)


def contract_rows(left, right):
    return lax.dot_general(
        left, right, (((0,), (0,)), ((), ())), preferred_element_type=jnp.float32
    )


def shards(
    activations, cotangent, route_ids, route_weights, gate_weights, up_weights, down_weights
):
    tok_rows, width = activations.shape
    topk = route_ids.shape[1]
    num_dp = lax.axis_size("dp")
    num_exp = lax.axis_size("expert")
    slice_width = gate_weights.shape[1]
    hidden = gate_weights.shape[2]
    capacity = min(tok_rows, 5 * tok_rows * topk // (4 * num_exp))
    buffer_rows = num_exp * num_dp * capacity
    flat_ids = route_ids.reshape(-1)
    expert_iota = jnp.arange(num_exp, dtype=jnp.int32)
    onehot = (flat_ids[:, None] == expert_iota[None, :]).astype(jnp.int32)
    before = jnp.cumsum(onehot, axis=0) - onehot
    slot = jnp.sum(before * onehot, axis=1)
    target = (flat_ids * capacity + slot).reshape(tok_rows, topk)
    slot_iota = jnp.arange(num_exp * capacity, dtype=jnp.int32)
    matches = target[:, :, None] == slot_iota[None, None, :]
    placing = jnp.any(matches, axis=1).astype(jnp.bfloat16)
    slot_weight = jnp.sum(jnp.where(matches, route_weights[:, :, None], 0.0), axis=(0, 1))
    send_act = contract_rows(placing, activations).astype(jnp.bfloat16)
    send_cot = (contract_rows(placing, cotangent) * slot_weight[:, None]).astype(jnp.bfloat16)
    send_act = send_act.reshape(num_exp, capacity, num_dp, slice_width)
    send_cot = send_cot.reshape(num_exp, capacity, num_dp, slice_width)
    flat_act = jnp.swapaxes(send_act, 1, 2).reshape(num_exp * num_dp, capacity, slice_width)
    flat_cot = jnp.swapaxes(send_cot, 1, 2).reshape(num_exp * num_dp, capacity, slice_width)
    recv_act, recv_cot = (
        lax.all_to_all(flat_act, ("expert", "dp"), split_axis=0, concat_axis=0, tiled=True),
        lax.all_to_all(flat_cot, ("expert", "dp"), split_axis=0, concat_axis=0, tiled=True),
    )
    recv_act = recv_act.reshape(buffer_rows, slice_width)
    recv_cot = recv_cot.reshape(buffer_rows, slice_width)
    gate_local = gate_weights[0]
    up_local = up_weights[0]
    down_local = down_weights[0]
    act_rows = recv_act
    cot_rows = recv_cot
    gate_part = jnp.dot(act_rows, gate_local, preferred_element_type=jnp.float32)
    up_part = jnp.dot(act_rows, up_local, preferred_element_type=jnp.float32)
    back_part = lax.dot_general(
        cot_rows, down_local, (((1,), (1,)), ((), ())), preferred_element_type=jnp.float32
    )
    summed = lax.psum(jnp.concatenate([gate_part, up_part, back_part], axis=1), "dp")
    grad_pre, grad_lin, activated = swiglu_back(
        summed[:, :hidden], summed[:, hidden : 2 * hidden], summed[:, 2 * hidden :]
    )
    act_rows = recv_act
    cot_rows = recv_cot
    rows_back = lax.dot_general(
        grad_pre, gate_local, (((1,), (1,)), ((), ())), preferred_element_type=jnp.float32
    ) + lax.dot_general(
        grad_lin, up_local, (((1,), (1,)), ((), ())), preferred_element_type=jnp.float32
    )
    grad_gate = contract_rows(act_rows, grad_pre).astype(jnp.bfloat16)[None]
    grad_up = contract_rows(act_rows, grad_lin).astype(jnp.bfloat16)[None]
    grad_down = contract_rows(activated, cot_rows).astype(jnp.bfloat16)[None]
    back_rows = rows_back.astype(jnp.bfloat16)
    flat_back = back_rows.reshape(num_exp * num_dp, capacity, slice_width)
    arrived = lax.all_to_all(flat_back, ("expert", "dp"), split_axis=0, concat_axis=0, tiled=True)
    arrived = jnp.swapaxes(arrived.reshape(num_exp, num_dp, capacity, slice_width), 1, 2)
    arrived = arrived.reshape(num_exp * capacity, width)
    grad_input = jnp.dot(placing, arrived, preferred_element_type=jnp.float32).astype(jnp.bfloat16)
    return (grad_input, grad_gate, grad_up, grad_down)


def solution(mesh):
    placed = (
        P(("expert", "dp"), None),
        P(("expert", "dp"), None),
        P(("expert", "dp"), None),
        P(("expert", "dp"), None),
        P("expert", "dp", None),
        P("expert", "dp", None),
        P("expert", None, "dp"),
    )
    return jax.shard_map(
        shards,
        mesh=mesh,
        in_specs=placed,
        out_specs=(
            P(("expert", "dp"), None),
            P("expert", "dp", None),
            P("expert", "dp", None),
            P("expert", None, "dp"),
        ),
        check_vma=False,
    )
```

profile of v0, /device:TPU:1, one launch (start us, length us, event | category | flops | bytes accessed | tf_op | source)
XLA Modules:
  0.0 371.8 jit_solution(10881495854793656829)
XLA Ops:
  7.2 0.0 copy-start
  7.2 0.8 copy.30
  8.0 0.1 eq.28
  8.1 0.1 fusion.19
  8.2 0.2 reduce_window_sum.11
  8.3 0.2 select_reduce_fusion.1
  8.5 0.1 reduce_sum.21
  8.6 0.1 fusion.18
  8.8 2.2 convolution_convert_fusion
  10.9 3.5 reshape.45
  14.4 2.5 copy.38
  16.9 11.9 %all-to-all-start = ((bf16[128,5,1792]{2,1,0:T(8,128)(2,1)}), bf16[128,5,1792]{2,1,0:T(8,128)(2,1)}, u32[]{:S(2)}, u32[]{:S(2)}) async-start(bf16[128,5,1792]{2,1,0:T(8,128)(2,1)} %bitcast.49), calls=%async_computation | async-start | bytes 7340032 | tf_op jit(solution)/shard_map/all_to_all | solution.py:50
  28.8 0.1 copy.34
  28.9 0.1 select_reduce_fusion
  29.0 0.8 fusion
  29.8 2.9 reshape.48
  32.8 4.2 %copy.39 = bf16[32,4,5,1792]{3,2,1,0:T(8,128)(2,1)} copy(bf16[32,4,5,1792]{3,1,2,0:T(4,128)(2,1)} %bitcast.52) | data formatting | bytes 4587520 | tf_op jit(solution)/shard_map/reshape | solution.py:48
  36.9 39.4 %all-to-all-done = bf16[128,5,1792]{2,1,0:T(8,128)(2,1)} async-done(((bf16[128,5,1792]{2,1,0:T(8,128)(2,1)}), bf16[128,5,1792]{2,1,0:T(8,128)(2,1)}, u32[]{:S(2)}, u32[]{:S(2)}) %all-to-all-start) | async-done | bytes 2293792 | tf_op jit(solution)/shard_map/all_to_all | solution.py:50
  76.4 4.7 %all-to-all-start.1 = ((bf16[128,5,1792]{2,1,0:T(8,128)(2,1)}), bf16[128,5,1792]{2,1,0:T(8,128)(2,1)}, u32[]{:S(2)}, u32[]{:S(2)}) async-start(bf16[128,5,1792]{2,1,0:T(8,128)(2,1)} %bitcast.48), calls=%async_computation.1 | async-start | bytes 7340032 | tf_op jit(solution)/shard_map/all_to_all | solution.py:51
  81.1 0.2 all-reduce.2.cloned.1.call-start
  81.3 5.4 %reshape.47 = bf16[640,1792]{1,0:T(8,128)(2,1)} reshape(bf16[128,5,1792]{2,1,0:T(8,128)(2,1)} %all-to-all-done) | data formatting | bytes 4587520 | tf_op jit(solution)/shard_map/reshape | solution.py:53
  86.7 5.4 %fusion.5 = f32[640,1024]{1,0:T(8,128)S(1)} fusion(bf16[640,1792]{1,0:T(8,128)(2,1)} %reshape.47, bf16[1,1792,1024]{2,1,0:T(8,128)(2,1)} %param.12), kind=kOutput, calls=%fused_computation.13 | convolution fusion | flops 2348810240 | bytes 8585216 | tf_op jit(solution)/shard_map/dot_general | solution.py:61
  92.1 4.0 %fusion.9 = f32[640,1024]{1,0:T(8,128)} fusion(bf16[640,1792]{1,0:T(8,128)(2,1)S(1)} %copy-done.3, bf16[1,1792,1024]{2,1,0:T(8,128)(2,1)S(1)} %copy-done.12), kind=kOutput, calls=%fused_computation.17 | convolution fusion | flops 2348810240 | bytes 8585216 | tf_op jit(solution)/shard_map/dot_general | solution.py:60
  96.1 32.5 %all-to-all-done.1 = bf16[128,5,1792]{2,1,0:T(8,128)(2,1)} async-done(((bf16[128,5,1792]{2,1,0:T(8,128)(2,1)}), bf16[128,5,1792]{2,1,0:T(8,128)(2,1)}, u32[]{:S(2)}, u32[]{:S(2)}) %all-to-all-start.1) | async-done | bytes 2293792 | tf_op jit(solution)/shard_map/all_to_all | solution.py:51
  128.6 5.4 %reshape.50 = bf16[640,1792]{1,0:T(8,128)(2,1)} reshape(bf16[128,5,1792]{2,1,0:T(8,128)(2,1)} %all-to-all-done.1) | data formatting | bytes 4587520 | tf_op jit(solution)/shard_map/reshape | solution.py:54
  134.0 5.4 %fusion.1 = f32[640,1024]{1,0:T(8,128)S(1)} fusion(bf16[640,1792]{1,0:T(8,128)(2,1)} %reshape.50, bf16[1,1024,1792]{2,1,0:T(8,128)(2,1)} %param.13), kind=kOutput, calls=%fused_computation.9 | convolution fusion | flops 2348810240 | bytes 8585216 | tf_op jit(solution)/shard_map/dot_general | solution.py:62
  139.5 3.5 pad_maximum_fusion
  142.9 0.0 all-reduce.2.cloned.1.call-update
  142.9 147.8 %all-reduce.2.cloned.1.call-done = f32[640,3072]{1,0:T(8,128)} async-done(((f32[640,3072]{1,0:T(8,128)}), f32[640,3072]{1,0:T(8,128)}) %all-reduce.2.cloned.1.call-update) | async-done | bytes 7864336 | tf_op jit(solution)/shard_map/psum | solution.py:65
  290.7 5.0 %multiply_convert_fusion.2 = (bf16[640,1024]{1,0:T(8,128)(2,1)S(1)}, bf16[640,1024]{1,0:T(8,128)(2,1)S(1)}) fusion(f32[640,3072]{1,0:T(8,128)} %all-reduce.2.cloned.1.call-done), kind=kLoop, calls=%fused_computation.24 | loop fusion | flops 8519680 | bytes 10485760 | tf_op jit(solution)/shard_map/convert_element_type | solution.py:11
  295.7 0.0 copy-start.8
  295.8 0.0 copy-done.11
  295.8 0.0 copy-start.13
  295.8 2.6 fusion.3
  298.4 0.3 copy-done.13
  298.7 2.6 add_convert_fusion
  301.3 2.7 reshape.51
  304.1 8.9 %all-to-all-start.2 = ((bf16[128,5,1792]{2,1,0:T(8,128)(2,1)}), bf16[128,5,1792]{2,1,0:T(8,128)(2,1)}, u32[]{:S(2)}, u32[]{:S(2)}) async-start(bf16[128,5,1792]{2,1,0:T(8,128)(2,1)} %reshape.51), calls=%async_computation.2 | async-start | bytes 7340032 | tf_op jit(solution)/shard_map/all_to_all | solution.py:81
  313.0 5.9 %fusion.11 = bf16[1,1792,1024]{2,1,0:T(8,128)(2,1)} fusion(bf16[640,1792]{1,0:T(8,128)(2,1)S(1)} %copy-done.4, bf16[640,1024]{1,0:T(8,128)(2,1)} %copy-done.8), kind=kOutput, calls=%fused_computation.19 | convolution fusion | flops 2350645248 | bytes 7274496 | tf_op jit(solution)/shard_map/dot_general | solution.py:17
  318.9 0.0 copy-done.7
  318.9 4.5 %fusion.12 = bf16[1,1792,1024]{2,1,0:T(8,128)(2,1)} fusion(bf16[640,1792]{1,0:T(8,128)(2,1)S(1)} %copy-done.4, bf16[640,1024]{1,0:T(8,128)(2,1)S(1)} %copy-done.7), kind=kOutput, calls=%fused_computation.20 | convolution fusion | flops 2350645248 | bytes 7274496 | tf_op jit(solution)/shard_map/dot_general | solution.py:17
  323.5 0.0 copy-done.5
  323.5 7.6 %fusion.13 = bf16[1,1024,1792]{2,1,0:T(8,128)(2,1)} fusion(bf16[640,1792]{1,0:T(8,128)(2,1)S(1)} %copy-done.5, f32[640,3072]{1,0:T(8,128)} %all-reduce.2.cloned.1.call-done), kind=kOutput, calls=%fused_computation.21 | convolution fusion | flops 2354577408 | bytes 11206656 | tf_op jit(solution)/shard_map/dot_general | solution.py:17
  331.1 29.4 %all-to-all-done.2 = bf16[128,5,1792]{2,1,0:T(8,128)(2,1)} async-done(((bf16[128,5,1792]{2,1,0:T(8,128)(2,1)}), bf16[128,5,1792]{2,1,0:T(8,128)(2,1)}, u32[]{:S(2)}, u32[]{:S(2)}) %all-to-all-start.2) | async-done | bytes 2293792 | tf_op jit(solution)/shard_map/all_to_all | solution.py:81
  360.5 3.0 copy.37
  363.5 0.0 copy-start.1
  363.5 0.3 copy.42
  363.8 1.1 convolution_convert_fusion.1
  (21 shorter events, 0.1 us)
Async XLA Ops:
  7.2 1.6 copy-start
  16.9 11.9 %copy-start.10 = (f32[16,8]{0,1:T(8,128)S(1)}, f32[16,8]{0,1:T(8,128)}, u32[]{:S(2)}) copy-start(f32[16,8]{0,1:T(8,128)} %param.10) | copy-start | bytes 1540
  16.9 12.1 %copy-start.9 = (bf16[16,7168]{1,0:T(8,128)(2,1)S(1)}, bf16[16,7168]{1,0:T(8,128)(2,1)}, u32[]{:S(2)}) copy-start(bf16[16,7168]{1,0:T(8,128)(2,1)} %param.8) | copy-start | bytes 688132
  16.9 59.4 %all-to-all-start = ((bf16[128,5,1792]{2,1,0:T(8,128)(2,1)}), bf16[128,5,1792]{2,1,0:T(8,128)(2,1)}, u32[]{:S(2)}, u32[]{:S(2)}) async-start(bf16[128,5,1792]{2,1,0:T(8,128)(2,1)} %bitcast.49), calls=%async_computation | async-start | bytes 7340032 | tf_op jit(solution)/shard_map/all_to_all | solution.py:50
  76.4 52.3 %all-to-all-start.1 = ((bf16[128,5,1792]{2,1,0:T(8,128)(2,1)}), bf16[128,5,1792]{2,1,0:T(8,128)(2,1)}, u32[]{:S(2)}, u32[]{:S(2)}) async-start(bf16[128,5,1792]{2,1,0:T(8,128)(2,1)} %bitcast.48), calls=%async_computation.1 | async-start | bytes 7340032 | tf_op jit(solution)/shard_map/all_to_all | solution.py:51
  81.1 209.7 %all-reduce.2.cloned.1.call-start = ((), (), s32[]{:S(2)}) async-start(), calls=%async_computation.3 | async-start | bytes 15728640 | tf_op jit(solution)/shard_map/psum | solution.py:65
  86.7 5.4 %copy-start.3 = (bf16[640,1792]{1,0:T(8,128)(2,1)S(1)}, bf16[640,1792]{1,0:T(8,128)(2,1)}, u32[]{:S(2)}) copy-start(bf16[640,1792]{1,0:T(8,128)(2,1)} %reshape.47) | copy-start | bytes 6881284
  86.7 5.4 %copy-start.12 = (bf16[1,1792,1024]{2,1,0:T(8,128)(2,1)S(1)}, bf16[1,1792,1024]{2,1,0:T(8,128)(2,1)}, u32[]{:S(2)}) copy-start(bf16[1,1792,1024]{2,1,0:T(8,128)(2,1)} %param.11) | copy-start | bytes 11010052
  134.0 5.4 %copy-start.2 = (f32[640,1024]{1,0:T(8,128)S(1)}, f32[640,1024]{1,0:T(8,128)}, u32[]{:S(2)}) copy-start(f32[640,1024]{1,0:T(8,128)} %fusion.9) | copy-start | bytes 7864324
  290.7 5.1 %copy-start.11 = (bf16[1,1792,1024]{2,1,0:T(8,128)(2,1)S(1)}, bf16[1,1792,1024]{2,1,0:T(8,128)(2,1)}, u32[]{:S(2)}) copy-start(bf16[1,1792,1024]{2,1,0:T(8,128)(2,1)} %param.12) | copy-start | bytes 11010052
  295.7 2.6 copy-start.6
  295.7 2.6 copy-start.8
  295.8 3.0 copy-start.13
  304.1 8.9 %copy-start.4 = (bf16[640,1792]{1,0:T(8,128)(2,1)S(1)}, bf16[640,1792]{1,0:T(8,128)(2,1)}, u32[]{:S(2)}) copy-start(bf16[640,1792]{1,0:T(8,128)(2,1)} %reshape.47) | copy-start | bytes 6881284
  304.1 56.4 %all-to-all-start.2 = ((bf16[128,5,1792]{2,1,0:T(8,128)(2,1)}), bf16[128,5,1792]{2,1,0:T(8,128)(2,1)}, u32[]{:S(2)}, u32[]{:S(2)}) async-start(bf16[128,5,1792]{2,1,0:T(8,128)(2,1)} %reshape.51), calls=%async_computation.2 | async-start | bytes 7340032 | tf_op jit(solution)/shard_map/all_to_all | solution.py:81
  313.0 6.0 %copy-start.7 = (bf16[640,1024]{1,0:T(8,128)(2,1)S(1)}, bf16[640,1024]{1,0:T(8,128)(2,1)}, u32[]{:S(2)}) copy-start(bf16[640,1024]{1,0:T(8,128)(2,1)} %copy-done.6) | copy-start | bytes 3932164
  318.9 4.5 %copy-start.5 = (bf16[640,1792]{1,0:T(8,128)(2,1)S(1)}, bf16[640,1792]{1,0:T(8,128)(2,1)}, u32[]{:S(2)}) copy-start(bf16[640,1792]{1,0:T(8,128)(2,1)} %reshape.50) | copy-start | bytes 6881284
  363.5 1.4 copy-start.1
Sparse Core Ops, SparseCore 0:
  143.1 147.5 all-reduce.1
where the time goes:
time: 373 us; the launch traced here: 372 us
  waiting for transfers between devices  249 us (67%)
  matrix products  42.2 us (11%)
  local copies, waits for them, and re-layouts  31.3 us (8%)
  starting transfers between devices  25.7 us (7%)
  between operations  14.3 us (4%)
  other arithmetic  9.16 us (2%)
    psum x1, waiting for transfers between devices, shards(): lax.psum(jnp.concatenate([gate_part, up_part, back_part], axis=1), 'dp')  148 us
    all_to_all x1, waiting for transfers between devices, shards(): lax.all_to_all(flat_act, ('expert', 'dp'), split_axis=0, concat_axis=0, t...  39.4 us
    all_to_all x1, waiting for transfers between devices, shards(): lax.all_to_all(flat_cot, ('expert', 'dp'), split_axis=0, concat_axis=0, t...  32.5 us
    all_to_all x1, waiting for transfers between devices, shards(): lax.all_to_all(flat_back, ('expert', 'dp'), split_axis=0, concat_axis=0,...  29.4 us
    dot_general x5, matrix products, contract_rows(): lax.dot_general(left, right, (((0,), (0,)), ((), ())), preferred_element_...  21.1 us
    all_to_all x1, starting transfers between devices, shards(): lax.all_to_all(flat_act, ('expert', 'dp'), split_axis=0, concat_axis=0, t...  11.9 us
    all_to_all x1, starting transfers between devices, shards(): lax.all_to_all(flat_back, ('expert', 'dp'), split_axis=0, concat_axis=0,...  8.88 us
  transfers between devices with their start and end apart: 4, of which 4 were waited for; matrix products, arithmetic and copies ran while one was open for 11% of the time, Pallas kernels for 0%

commit v1 on v0

--- a/solution.py
+++ b/solution.py
@@ -62,7 +62,9 @@
     back_part = lax.dot_general(
         cot_rows, down_local, (((1,), (1,)), ((), ())), preferred_element_type=jnp.float32
     )
-    summed = lax.psum(jnp.concatenate([gate_part, up_part, back_part], axis=1), "dp")
+    summed = jnp.sum(
+        lax.all_gather(jnp.concatenate([gate_part, up_part, back_part], axis=1), "dp"), axis=0
+    )
     grad_pre, grad_lin, activated = swiglu_back(
         summed[:, :hidden], summed[:, hidden : 2 * hidden], summed[:, 2 * hidden :]
     )

time: 373 us -> 513 us (1.38)
  waiting for transfers between devices: 249 us -> 373 us
  other arithmetic: 9.16 us -> 24.3 us
    all_gather x0 -> x1, waiting for transfers between devices: none -> 271 us  [shards(): lax.all_gather(jnp.concatenate([gate_part, up_part, back_part], axis=1),...]
    psum x1 -> x0, waiting for transfers between devices: 148 us -> none  [shards(): lax.psum(jnp.concatenate([gate_part, up_part, back_part], axis=1), 'dp')]
    reduce_sum x0 -> x1, other arithmetic: none -> 15.1 us  [shards(): jnp.sum(lax.all_gather(jnp.concatenate([gate_part, up_part, back_part], a...]
  transfers between devices with their start and end apart: 4 -> 4, of which waited for: 4 -> 4; matrix products, arithmetic and copies ran while one was open for 11% -> 8% of each run, Pallas kernels for 0% -> 0%
where the time goes in v1:
time: 513 us; the launch traced here: 512 us
  waiting for transfers between devices  373 us (73%)
  matrix products  42.3 us (8%)
  local copies, waits for them, and re-layouts  31.5 us (6%)
  starting transfers between devices  26.6 us (5%)
  other arithmetic  24.3 us (5%)
  between operations  14.3 us (3%)
    all_gather x1, waiting for transfers between devices, shards(): lax.all_gather(jnp.concatenate([gate_part, up_part, back_part], axis=1),...  271 us
    all_to_all x1, waiting for transfers between devices, shards(): lax.all_to_all(flat_act, ('expert', 'dp'), split_axis=0, concat_axis=0, t...  39.4 us
    all_to_all x1, waiting for transfers between devices, shards(): lax.all_to_all(flat_cot, ('expert', 'dp'), split_axis=0, concat_axis=0, t...  32.5 us
    all_to_all x1, waiting for transfers between devices, shards(): lax.all_to_all(flat_back, ('expert', 'dp'), split_axis=0, concat_axis=0,...  29.4 us
    dot_general x5, matrix products, contract_rows(): lax.dot_general(left, right, (((0,), (0,)), ((), ())), preferred_element_...  21.1 us
    reduce_sum x1, other arithmetic, shards(): jnp.sum(lax.all_gather(jnp.concatenate([gate_part, up_part, back_part], a...  15.1 us
    all_to_all x1, starting transfers between devices, shards(): lax.all_to_all(flat_act, ('expert', 'dp'), split_axis=0, concat_axis=0, t...  11.9 us
  transfers between devices with their start and end apart: 4, of which 4 were waited for; matrix products, arithmetic and copies ran while one was open for 8% of the time, Pallas kernels for 0%

profile of v1, /device:TPU:1, one launch (start us, length us, event | category | flops | bytes accessed | tf_op | source)
XLA Modules:
  0.0 511.7 jit_solution(5905297552611053820)
XLA Ops:
  7.2 0.0 copy-start
  7.2 0.8 copy.30
  8.0 0.1 eq.28
  8.1 0.1 fusion.19
  8.2 0.2 reduce_window_sum.11
  8.3 0.2 select_reduce_fusion.1
  8.5 0.1 reduce_sum.30
  8.6 0.1 fusion.18
  8.8 2.2 convolution_convert_fusion
  10.9 3.5 reshape.45
  14.4 2.5 copy.38
  16.9 11.9 %all-to-all-start = ((bf16[128,5,1792]{2,1,0:T(8,128)(2,1)}), bf16[128,5,1792]{2,1,0:T(8,128)(2,1)}, u32[]{:S(2)}, u32[]{:S(2)}) async-start(bf16[128,5,1792]{2,1,0:T(8,128)(2,1)} %bitcast.51), calls=%async_computation | async-start | bytes 7340032 | tf_op jit(solution)/shard_map/all_to_all | solution.py:50
  28.8 0.1 copy.34
  28.9 0.1 select_reduce_fusion
  29.0 0.8 fusion
  29.8 2.9 reshape.48
  32.8 4.2 copy.39
  36.9 39.4 %all-to-all-done = bf16[128,5,1792]{2,1,0:T(8,128)(2,1)} async-done(((bf16[128,5,1792]{2,1,0:T(8,128)(2,1)}), bf16[128,5,1792]{2,1,0:T(8,128)(2,1)}, u32[]{:S(2)}, u32[]{:S(2)}) %all-to-all-start) | async-done | bytes 2293792 | tf_op jit(solution)/shard_map/all_to_all | solution.py:50
  76.4 4.7 all-to-all-start.1
  81.1 0.2 all-gather.3.cloned.1.call-start
  81.3 5.4 %reshape.47 = bf16[640,1792]{1,0:T(8,128)(2,1)} reshape(bf16[128,5,1792]{2,1,0:T(8,128)(2,1)} %all-to-all-done) | data formatting | bytes 4587520 | tf_op jit(solution)/shard_map/reshape | solution.py:53
  86.7 5.4 %fusion.5 = f32[640,1024]{1,0:T(8,128)S(1)} fusion(bf16[640,1792]{1,0:T(8,128)(2,1)} %reshape.47, bf16[1,1792,1024]{2,1,0:T(8,128)(2,1)} %param.12), kind=kOutput, calls=%fused_computation.13 | convolution fusion | flops 2348810240 | bytes 8585216 | tf_op jit(solution)/shard_map/dot_general | solution.py:61
  92.1 4.0 fusion.9
  96.1 32.5 %all-to-all-done.1 = bf16[128,5,1792]{2,1,0:T(8,128)(2,1)} async-done(((bf16[128,5,1792]{2,1,0:T(8,128)(2,1)}), bf16[128,5,1792]{2,1,0:T(8,128)(2,1)}, u32[]{:S(2)}, u32[]{:S(2)}) %all-to-all-start.1) | async-done | bytes 2293792 | tf_op jit(solution)/shard_map/all_to_all | solution.py:51
  128.6 5.4 %reshape.50 = bf16[640,1792]{1,0:T(8,128)(2,1)} reshape(bf16[128,5,1792]{2,1,0:T(8,128)(2,1)} %all-to-all-done.1) | data formatting | bytes 4587520 | tf_op jit(solution)/shard_map/reshape | solution.py:54
  134.0 5.4 %fusion.1 = f32[640,1024]{1,0:T(8,128)S(1)} fusion(bf16[640,1792]{1,0:T(8,128)(2,1)} %reshape.50, bf16[1,1024,1792]{2,1,0:T(8,128)(2,1)} %param.13), kind=kOutput, calls=%fused_computation.9 | convolution fusion | flops 2348810240 | bytes 8585216 | tf_op jit(solution)/shard_map/dot_general | solution.py:62
  139.5 3.4 pad_maximum_fusion
  142.9 0.0 all-gather.3.cloned.1.call-update
  142.9 271.5 %all-gather.3.cloned.1.call-done = f32[2560,3072]{1,0:T(8,128)} async-done(((f32[640,3072]{1,0:T(8,128)}), f32[2560,3072]{1,0:T(8,128)}) %all-gather.3.cloned.1.call-update) | async-done | bytes 31457296 | tf_op jit(solution)/shard_map/all_gather | solution.py:66
  414.4 15.1 %reduce_sum.32 = f32[640,3072]{1,0:T(8,128)} reduce(f32[4,640,3072]{2,1,0:T(8,128)} %bitcast.49, f32[]{:T(128)} %constant.12.clone.1), dimensions={0}, to_apply=%region_4.5 | reduce | flops 5898240 | bytes 39321604 | tf_op jit(solution)/shard_map/reduce_sum | solution.py:65
  429.5 5.0 multiply_convert_fusion.2
  434.6 0.0 copy-start.8
  434.6 0.0 copy-done.11
  434.6 0.0 copy-start.13
  434.6 2.6 fusion.3
  437.2 0.3 copy-done.13
  437.6 2.6 add_convert_fusion
  440.2 2.9 reshape.51
  443.1 9.8 %all-to-all-start.2 = ((bf16[128,5,1792]{2,1,0:T(8,128)(2,1)}), bf16[128,5,1792]{2,1,0:T(8,128)(2,1)}, u32[]{:S(2)}, u32[]{:S(2)}) async-start(bf16[128,5,1792]{2,1,0:T(8,128)(2,1)} %reshape.51), calls=%async_computation.2 | async-start | bytes 7340032 | tf_op jit(solution)/shard_map/all_to_all | solution.py:83
  452.9 0.0 copy-done.4
  453.0 5.9 %fusion.11 = bf16[1,1792,1024]{2,1,0:T(8,128)(2,1)} fusion(bf16[640,1792]{1,0:T(8,128)(2,1)S(1)} %copy-done.4, bf16[640,1024]{1,0:T(8,128)(2,1)} %copy-done.8), kind=kOutput, calls=%fused_computation.19 | convolution fusion | flops 2350645248 | bytes 7274496 | tf_op jit(solution)/shard_map/dot_general | solution.py:17
  458.9 4.5 fusion.12
  463.4 7.7 %fusion.13 = bf16[1,1024,1792]{2,1,0:T(8,128)(2,1)} fusion(bf16[640,1792]{1,0:T(8,128)(2,1)S(1)} %copy-done.5, f32[640,3072]{1,0:T(8,128)} %reduce_sum.32), kind=kOutput, calls=%fused_computation.21 | convolution fusion | flops 2354577408 | bytes 11206656 | tf_op jit(solution)/shard_map/dot_general | solution.py:17
  471.1 29.4 %all-to-all-done.2 = bf16[128,5,1792]{2,1,0:T(8,128)(2,1)} async-done(((bf16[128,5,1792]{2,1,0:T(8,128)(2,1)}), bf16[128,5,1792]{2,1,0:T(8,128)(2,1)}, u32[]{:S(2)}, u32[]{:S(2)}) %all-to-all-start.2) | async-done | bytes 2293792 | tf_op jit(solution)/shard_map/all_to_all | solution.py:83
  500.5 3.0 copy.37
  503.4 0.0 copy-start.1
  503.4 0.3 copy.42
  503.8 1.1 convolution_convert_fusion.1
  (22 shorter events, 0.1 us)
Async XLA Ops:
  7.2 1.6 copy-start
  16.9 11.9 %copy-start.10 = (f32[16,8]{0,1:T(8,128)S(1)}, f32[16,8]{0,1:T(8,128)}, u32[]{:S(2)}) copy-start(f32[16,8]{0,1:T(8,128)} %param.10) | copy-start | bytes 1540
  16.9 12.1 %copy-start.9 = (bf16[16,7168]{1,0:T(8,128)(2,1)S(1)}, bf16[16,7168]{1,0:T(8,128)(2,1)}, u32[]{:S(2)}) copy-start(bf16[16,7168]{1,0:T(8,128)(2,1)} %param.8) | copy-start | bytes 688132
  16.9 59.4 %all-to-all-start = ((bf16[128,5,1792]{2,1,0:T(8,128)(2,1)}), bf16[128,5,1792]{2,1,0:T(8,128)(2,1)}, u32[]{:S(2)}, u32[]{:S(2)}) async-start(bf16[128,5,1792]{2,1,0:T(8,128)(2,1)} %bitcast.51), calls=%async_computation | async-start | bytes 7340032 | tf_op jit(solution)/shard_map/all_to_all | solution.py:50
  76.4 52.3 %all-to-all-start.1 = ((bf16[128,5,1792]{2,1,0:T(8,128)(2,1)}), bf16[128,5,1792]{2,1,0:T(8,128)(2,1)}, u32[]{:S(2)}, u32[]{:S(2)}) async-start(bf16[128,5,1792]{2,1,0:T(8,128)(2,1)} %bitcast.50), calls=%async_computation.1 | async-start | bytes 7340032 | tf_op jit(solution)/shard_map/all_to_all | solution.py:51
  81.1 333.3 %all-gather.3.cloned.1.call-start = ((), (), s32[]{:S(2)}) async-start(), calls=%async_computation.3 | async-start | bytes 39321600 | tf_op jit(solution)/shard_map/all_gather | solution.py:66
  86.7 5.4 %copy-start.3 = (bf16[640,1792]{1,0:T(8,128)(2,1)S(1)}, bf16[640,1792]{1,0:T(8,128)(2,1)}, u32[]{:S(2)}) copy-start(bf16[640,1792]{1,0:T(8,128)(2,1)} %reshape.47) | copy-start | bytes 6881284
  86.7 5.4 %copy-start.12 = (bf16[1,1792,1024]{2,1,0:T(8,128)(2,1)S(1)}, bf16[1,1792,1024]{2,1,0:T(8,128)(2,1)}, u32[]{:S(2)}) copy-start(bf16[1,1792,1024]{2,1,0:T(8,128)(2,1)} %param.11) | copy-start | bytes 11010052
  134.0 5.4 %copy-start.2 = (f32[640,1024]{1,0:T(8,128)S(1)}, f32[640,1024]{1,0:T(8,128)}, u32[]{:S(2)}) copy-start(f32[640,1024]{1,0:T(8,128)} %fusion.9) | copy-start | bytes 7864324
  429.5 5.1 copy-start.11
  434.6 2.6 copy-start.6
  434.6 2.6 copy-start.8
  434.6 3.0 copy-start.13
  443.1 9.8 %copy-start.4 = (bf16[640,1792]{1,0:T(8,128)(2,1)S(1)}, bf16[640,1792]{1,0:T(8,128)(2,1)}, u32[]{:S(2)}) copy-start(bf16[640,1792]{1,0:T(8,128)(2,1)} %reshape.47) | copy-start | bytes 6881284
  443.1 57.4 %all-to-all-start.2 = ((bf16[128,5,1792]{2,1,0:T(8,128)(2,1)}), bf16[128,5,1792]{2,1,0:T(8,128)(2,1)}, u32[]{:S(2)}, u32[]{:S(2)}) async-start(bf16[128,5,1792]{2,1,0:T(8,128)(2,1)} %reshape.51), calls=%async_computation.2 | async-start | bytes 7340032 | tf_op jit(solution)/shard_map/all_to_all | solution.py:83
  452.9 6.0 %copy-start.7 = (bf16[640,1024]{1,0:T(8,128)(2,1)S(1)}, bf16[640,1024]{1,0:T(8,128)(2,1)}, u32[]{:S(2)}) copy-start(bf16[640,1024]{1,0:T(8,128)(2,1)} %copy-done.6) | copy-start | bytes 3932164
  458.9 4.5 copy-start.5
  503.4 1.4 copy-start.1
Sparse Core Ops, SparseCore 0:
  143.0 271.3 all-gather.2
